TPU v7x, 256 devices: a whole 4x4x8 slice. The times are simulated.
256 devices in a mesh: dp: 32 (over y, z_hi, core), tensor: 8 (over z_lo, x).
Axes of the slice: x: 4, y: 4, z: 8 (z_hi: 4, z_lo: 2; z = z_hi * 2 + z_lo), core: 2. Of those that a mesh axis runs over, the one named last changes fastest.
Arguments:
- inputs: bfloat16 [32768, 2048], P(('dp', 'tensor')), may hold values from -6 to 6
- norm_gain: float32 [2048], replicated, may hold values from 0.1 to 1.9
- proj_weight: bfloat16 [2048, 3, 2048], P('dp', None, 'tensor'), may hold values from -0.125 to 0.125
- filters: float32 [3, 7, 2048], P(None, None, 'tensor'), may hold values from -2.4 to 2.4
- cotangent: bfloat16 [32768, 2048], P('dp', 'tensor'), may hold values from -18 to 18
Outputs:
- mixed: bfloat16 [32768, 2048], P('dp', 'tensor')
- grad_inputs: bfloat16 [32768, 2048], P(('dp', 'tensor'))
- grad_proj: bfloat16 [2048, 3, 2048], P('dp', None, 'tensor')
- grad_filters: float32 [3, 7, 2048], P(None, None, 'tensor')
- grad_gain: float32 [2048], replicated
All inputs are finite; a program needn't handle non-finite values.
Results may differ from a plain program's by a relative error of at most 0.02.
Values may be sent and summed in bfloat16 or wider, within the bound.
No kernel may reach another device: no remote copies, remote signals or barrier semaphores. Data moves between devices by JAX's collectives and lax.ppermute only.
A program may use at most 64 MiB of HBM per device.

v0:
```python
import jax
import jax.numpy as jnp
from jax import lax
from jax.sharding import PartitionSpec as P


def passed_along(shard, axis, by):
    size = lax.axis_size(axis)
    pairs = [(i, i + by) for i in range(size) if 0 <= i + by < size]
    return lax.ppermute(shard, axis, pairs)


def body(inputs, norm_gain, proj_weight, filters, cotangent):
    taps = filters.shape[1]
    width = taps - 1
    wide = inputs.astype(jnp.float32)
    inv_rms = lax.rsqrt(jnp.mean(wide * wide, axis=1, keepdims=True) + 1e-05)
    normed = (wide * inv_rms * norm_gain).astype(jnp.bfloat16)
    weights = lax.all_gather(proj_weight, "dp", axis=0, tiled=True)
    positions = lax.all_gather(normed, "tensor", axis=0, tiled=True)
    length = positions.shape[0]
    streams = jnp.einsum(
        "td,dsc->tsc", positions, weights, preferred_element_type=jnp.float32
    ).astype(jnp.bfloat16)
    before = passed_along(streams[length - width :], "dp", 1)
    extended = jnp.concatenate([before, streams], axis=0).astype(jnp.float32)
    conv = jnp.zeros(streams.shape, jnp.float32)
    for tap in range(taps):
        conv = conv + filters[:, tap, :] * extended[width - tap : width - tap + length]
    mixed = (conv[:, 0] * conv[:, 1] * conv[:, 2]).astype(jnp.bfloat16)
    grad_out = cotangent.astype(jnp.float32)
    grad_conv = jnp.stack(
        [
            grad_out * conv[:, 1] * conv[:, 2],
            grad_out * conv[:, 0] * conv[:, 2],
            grad_out * conv[:, 0] * conv[:, 1],
        ],
        axis=1,
    )
    after = passed_along(grad_conv[:width], "dp", -1)
    grad_extended = jnp.concatenate([grad_conv, after], axis=0)
    grad_acc = jnp.zeros(streams.shape, jnp.float32)
    for tap in range(taps):
        grad_acc = grad_acc + filters[:, tap, :] * grad_extended[tap : tap + length]
    grad_streams = grad_acc.astype(jnp.bfloat16)
    filter_local = jnp.stack(
        [
            jnp.sum(grad_conv * extended[width - tap : width - tap + length], axis=0)
            for tap in range(taps)
        ],
        axis=1,
    )
    normed_terms = jnp.einsum(
        "tsc,dsc->td", grad_streams, weights, preferred_element_type=jnp.float32
    )
    grad_normed = lax.psum_scatter(
        normed_terms.astype(jnp.bfloat16), "tensor", scatter_dimension=0, tiled=True
    ).astype(jnp.float32)
    weight_terms = jnp.einsum(
        "td,tsc->dsc", positions, grad_streams, preferred_element_type=jnp.float32
    )
    grad_proj = lax.psum_scatter(
        weight_terms.astype(jnp.bfloat16), "dp", scatter_dimension=0, tiled=True
    )
    scaled = norm_gain * grad_normed
    grad_inputs = inv_rms * (
        scaled - wide * inv_rms * inv_rms * jnp.mean(scaled * wide, axis=1, keepdims=True)
    )
    gain_local = jnp.sum(grad_normed * wide * inv_rms, axis=0)
    grad_filters = lax.psum(filter_local, "dp")
    grad_gain = lax.psum(gain_local, ("dp", "tensor"))
    return (mixed, grad_inputs.astype(jnp.bfloat16), grad_proj, grad_filters, grad_gain)


def solution(mesh):
    return jax.shard_map(
        body,
        mesh=mesh,
        in_specs=(
            P(("dp", "tensor"), None),
            P(),
            P("dp", None, "tensor"),
            P(None, None, "tensor"),
            P("dp", "tensor"),
        ),
        out_specs=(
            P("dp", "tensor"),
            P(("dp", "tensor"), None),
            P("dp", None, "tensor"),
            P(None, None, "tensor"),
            P(),
        ),
        check_vma=False,
    )
```

profile of v0, /device:TPU:1, one launch (start us, length us, event | category | flops | bytes accessed | tf_op | source)
XLA Modules:
  0.0 393.9 jit_solution(4973453960555978686)
XLA Ops:
  7.2 0.0 all-gather.5.cloned.1.call-start
  7.2 0.7 all-gather.5.cloned.1.call-update
  7.9 0.0 all-gather.3.cloned.1.call-start
  7.9 1.2 fusion.26
  9.2 2.0 fusion.20
  11.2 0.0 all-gather.3.cloned.1.call-update
  11.2 0.0 reduce-scatter.3.cloned.1.call-start
  11.3 1.0 fusion.30
  12.3 59.7 %all-gather.5.cloned.1.call-done = bf16[2048,3,256]{2,0,1:T(8,128)(2,1)} async-done(((bf16[64,3,256]{2,0,1:T(8,128)(2,1)}), bf16[2048,3,256]{2,0,1:T(8,128)(2,1)}) %all-gather.5.cloned.1.call-update) | async-done | bytes 3145744 | tf_op jit(solution)/shard_map/all_gather | solution.py:19
  72.0 54.9 %all-gather.3.cloned.1.call-done = bf16[1024,2048]{1,0:T(8,128)(2,1)} async-done(((bf16[128,2048]{1,0:T(8,128)(2,1)}), bf16[1024,2048]{1,0:T(8,128)(2,1)}) %all-gather.3.cloned.1.call-update) | async-done | bytes 4194320 | tf_op jit(solution)/shard_map/all_gather | solution.py:20
  126.9 6.6 %fusion.14 = bf16[1024,3,256]{2,0,1:T(8,128)(2,1)S(1)} fusion(bf16[2048,3,256]{2,0,1:T(8,128)(2,1)} %all-gather.5.cloned.1.call-done, bf16[1024,2048]{1,0:T(8,128)(2,1)} %all-gather.3.cloned.1.call-done), kind=kOutput, calls=%fused_computation.33 | convolution fusion | flops 3222011904 | bytes 8912896 | tf_op jit(solution)/shard_map/td,dsc->tsc/dot_general | solution.py:22
  133.5 4.7 %collective-permute-start = (bf16[6,3,256]{2,0,1:T(8,128)(2,1)S(1)}, bf16[6,3,256]{2,0,1:T(8,128)(2,1)S(1)}, u32[]{:S(2)}, u32[]{:S(2)}) collective-permute-start(bf16[6,3,256]{2,0,1:T(8,128)(2,1)S(1)} %slice.120), channel_id=1, source_target_pairs={{0,8},{8,16},{16,24},{24,32},{32,40},{40,48},{48,56},{56,64},{64,7... | collective-permute-start | bytes 27656 | tf_op jit(solution)/shard_map/ppermute | solution.py:10
  138.3 0.8 collective-permute-done
  139.1 0.3 maximum_convert_fusion
  139.4 0.0 copy-start.1
  139.4 2.6 multiply_add_fusion
  142.0 1.2 fusion.25
  143.2 2.9 multiply_reduce_fusion
  146.0 1.9 collective-permute-start.1
  148.0 4.8 %collective-permute-done.1 = f32[6,3,256]{2,0,1:T(8,128)S(1)} collective-permute-done((f32[6,3,256]{2,0,1:T(8,128)S(1)}, f32[6,3,256]{2,0,1:T(8,128)S(1)}, u32[]{:S(2)}, u32[]{:S(2)}) %collective-permute-start.1) | collective-permute-done | bytes 18464 | tf_op jit(solution)/shard_map/ppermute | solution.py:10
  152.8 0.2 pad_maximum_fusion
  153.0 2.7 fusion.8
  155.8 5.1 %bitcast_convert_fusion = bf16[1024,2048]{1,0:T(8,128)(2,1)} fusion(bf16[1024,3,256]{2,0,1:T(8,128)(2,1)S(1)} %fusion.8, bf16[2048,3,256]{2,0,1:T(8,128)(2,1)S(1)} %copy-done.3), kind=kOutput, calls=%fused_computation | convolution fusion | flops 3223322624 | bytes 8912896 | tf_op jit(solution)/shard_map/tsc,dsc->td/dot_general | solution.py:53
  160.8 0.0 reduce-scatter.3.cloned.1.call-update
  160.9 0.2 reduce-scatter.5.cloned.1.call-start
  161.1 7.5 %fusion.4 = bf16[2048,3,256]{2,0,1:T(8,128)(2,1)} fusion(bf16[1024,3,256]{2,0,1:T(8,128)(2,1)S(1)} %fusion.8, bf16[1024,2048]{1,0:T(8,128)(2,1)} %all-gather.3.cloned.1.call-done), kind=kOutput, calls=%fused_computation.5 | convolution fusion | flops 3222798336 | bytes 8912896 | tf_op jit(solution)/shard_map/td,tsc->dsc/dot_general | solution.py:59
  168.6 0.0 reduce-scatter.5.cloned.1.call-update
  168.7 135.1 %psum.14 = f32[3,7,256]{2,0,1:T(4,128)S(1)} all-reduce(f32[3,7,256]{2,0,1:T(4,128)S(1)} %constant_dynamic-update-slice_fusion), channel_id=1, replica_groups=mesh['dp'=32,'tensor'=8] {'dp'}, use_global_device_ids=true, to_apply=%region_11.0 | all-reduce | flops 5376 | bytes 43008 | tf_op jit(solution)/shard_map/psum | solution.py:70
  303.8 0.6 copy.12
  304.5 1.4 fusion.29
  305.8 79.3 %psum.15 = f32[2048]{0:T(1024)} all-reduce(f32[2048]{0:T(1024)S(1)} %get-tuple-element.17), channel_id=1, replica_groups=mesh['dp'=32,'tensor'=8] {'dp','tensor'}, use_global_device_ids=true, to_apply=%region_13.0 | all-reduce | flops 2048 | bytes 16384 | tf_op jit(solution)/shard_map/psum | solution.py:71
  385.2 2.2 fusion.23
  (24 shorter events, 0.1 us)
Async XLA Ops:
  7.2 64.9 %all-gather.5.cloned.1.call-start = ((), (), s32[]{:S(2)}) async-start(), calls=%async_computation.3 | async-start | bytes 3244032 | tf_op jit(solution)/shard_map/all_gather | solution.py:19
  7.9 119.0 %all-gather.3.cloned.1.call-start = ((), (), s32[]{:S(2)}) async-start(), calls=%async_computation.2 | async-start | bytes 4718592 | tf_op jit(solution)/shard_map/all_gather | solution.py:20
  11.2 293.2 %reduce-scatter.3.cloned.1.call-start = ((), (), s32[]{:S(2)}) async-start(), calls=%async_computation.4 | async-start | bytes 4718592 | tf_op jit(solution)/shard_map/reduce_scatter | solution.py:56
  133.5 5.5 %collective-permute-start = (bf16[6,3,256]{2,0,1:T(8,128)(2,1)S(1)}, bf16[6,3,256]{2,0,1:T(8,128)(2,1)S(1)}, u32[]{:S(2)}, u32[]{:S(2)}) collective-permute-start(bf16[6,3,256]{2,0,1:T(8,128)(2,1)S(1)} %slice.120), channel_id=1, source_target_pairs={{0,8},{8,16},{16,24},{24,32},{32,40},{40,48},{48,56},{56,64},{64,7... | collective-permute-start | bytes 27656 | tf_op jit(solution)/shard_map/ppermute | solution.py:10
  139.4 2.6 copy-start.1
  146.0 6.8 %collective-permute-start.1 = (f32[6,3,256]{2,0,1:T(8,128)S(1)}, f32[6,3,256]{2,0,1:T(8,128)S(1)}, u32[]{:S(2)}, u32[]{:S(2)}) collective-permute-start(f32[6,3,256]{2,0,1:T(8,128)S(1)} %slice.131), channel_id=1, source_target_pairs={{8,0},{16,8},{24,16},{32,24},{40,32},{48,40},{56,48},{64,56},{72,6... | collective-permute-start | bytes 55304 | tf_op jit(solution)/shard_map/ppermute | solution.py:10
  153.0 2.7 copy-start.3
  160.9 226.5 %reduce-scatter.5.cloned.1.call-start = ((), (), s32[]{:S(2)}) async-start(), calls=%async_computation.5 | async-start | bytes 3244032 | tf_op jit(solution)/shard_map/reduce_scatter | solution.py:62
  168.6 135.8 %copy-start = (bf16[128,2048]{1,0:T(8,128)(2,1)S(1)}, bf16[128,2048]{1,0:T(8,128)(2,1)}, u32[]{:S(2)}) copy-start(bf16[128,2048]{1,0:T(8,128)(2,1)} %param.5) | copy-start | bytes 1572868
  168.6 135.8 %copy-start.2 = (f32[2048]{0:T(1024)S(1)}, f32[2048]{0:T(1024)}, u32[]{:S(2)}) copy-start(f32[2048]{0:T(1024)} %param.6) | copy-start | bytes 24580
Sparse Core Ops, SparseCore 0:
  10.7 61.3 all-gather.4
  74.4 52.5 all-gather.2
  161.0 54.1 reduce-scatter.2
  219.5 92.7 reduce-scatter.4
where the time goes:
time: 394 us
  blocking collectives  214 us (54%)
  waiting for transfers between devices  121 us (31%)
  matrix products  19.2 us (5%)
  other arithmetic  16.6 us (4%)
  between operations  13.9 us (4%)
  starting transfers between devices  6.99 us (2%)
    psum x1, blocking collectives, body(): grad_filters = lax.psum(filter_local, 'dp')  135 us
    psum x1, blocking collectives, body(): grad_gain = lax.psum(gain_local, ('dp', 'tensor'))  79.3 us
    all_gather x1, waiting for transfers between devices, body(): weights = lax.all_gather(proj_weight, 'dp', axis=0, tiled=True)  59.7 us
    all_gather x1, waiting for transfers between devices, body(): positions = lax.all_gather(normed, 'tensor', axis=0, tiled=True)  54.9 us
  transfers between devices with their start and end apart: 6, of which 4 were waited for; matrix products, arithmetic and copies ran while one was open for 4% of the time, Pallas kernels for 0%

commit v1 on v0

--- a/solution.py
+++ b/solution.py
@@ -68,7 +68,7 @@
     )
     gain_local = jnp.sum(grad_normed * wide * inv_rms, axis=0)
     grad_filters = lax.psum(filter_local, "dp")
-    grad_gain = lax.psum(gain_local, ("dp", "tensor"))
+    grad_gain = jnp.sum(lax.all_gather(gain_local, ("dp", "tensor")), axis=0)
     return (mixed, grad_inputs.astype(jnp.bfloat16), grad_proj, grad_filters, grad_gain)
 
 

time: 394 us -> 1020 us (2.59)
  waiting for transfers between devices: 121 us -> 816 us
  blocking collectives: 214 us -> 137 us
    all_gather x0 -> x1, waiting for transfers between devices: none -> 548 us  [body(): grad_gain = jnp.sum(lax.all_gather(gain_local, ('dp', 'tensor')), axis=0)]
    reduce_scatter x1, waiting for transfers between devices: 0.01 us -> 94.1 us  [body(): lax.psum_scatter(weight_terms.astype(jnp.bfloat16), 'dp', scatter_dimensi...]
    psum x1 -> x0, blocking collectives: 79.3 us -> none  [body(): grad_gain = lax.psum(gain_local, ('dp', 'tensor'))]
    reduce_scatter x1, waiting for transfers between devices: 0.01 us -> 53.4 us  [body(): lax.psum_scatter(normed_terms.astype(jnp.bfloat16), 'tensor', scatter_dim...]
  transfers between devices with their start and end apart: 6 -> 7, of which waited for: 4 -> 7; matrix products, arithmetic and copies ran while one was open for 4% -> 2% of each run, Pallas kernels for 0% -> 0%
where the time goes in v1:
time: 1020 us; the launch traced here: 1010 us
  waiting for transfers between devices  816 us (80%)
  blocking collectives  137 us (13%)
  matrix products  19.1 us (2%)
  other arithmetic  16.9 us (2%)
  between operations  14 us (1%)
    all_gather x1, waiting for transfers between devices, body(): grad_gain = jnp.sum(lax.all_gather(gain_local, ('dp', 'tensor')), axis=0)  548 us
    psum x1, blocking collectives, body(): grad_filters = lax.psum(filter_local, 'dp')  137 us
    reduce_scatter x1, waiting for transfers between devices, body(): lax.psum_scatter(weight_terms.astype(jnp.bfloat16), 'dp', scatter_dimensi...  94.1 us
    all_gather x1, waiting for transfers between devices, body(): weights = lax.all_gather(proj_weight, 'dp', axis=0, tiled=True)  59.7 us
    all_gather x1, waiting for transfers between devices, body(): positions = lax.all_gather(normed, 'tensor', axis=0, tiled=True)  54.9 us
    reduce_scatter x1, waiting for transfers between devices, body(): lax.psum_scatter(normed_terms.astype(jnp.bfloat16), 'tensor', scatter_dim...  53.4 us
  transfers between devices with their start and end apart: 7, of which 7 were waited for; matrix products, arithmetic and copies ran while one was open for 2% of the time, Pallas kernels for 0%

profile of v1, /device:TPU:1, one launch (start us, length us, event | category | flops | bytes accessed | tf_op | source)
XLA Modules:
  0.0 1014.1 jit_solution(13233797212724266496)
XLA Ops:
  7.2 0.7 all-gather.7.cloned.1.call-update
  7.9 0.0 all-gather.5.cloned.1.call-start
  7.9 1.2 fusion.26
  9.2 2.0 fusion.20
  11.2 0.0 reduce-scatter.3.cloned.1.call-start
  11.3 1.0 fusion.30
  12.3 59.7 %all-gather.7.cloned.1.call-done = bf16[2048,3,256]{2,0,1:T(8,128)(2,1)} async-done(((bf16[64,3,256]{2,0,1:T(8,128)(2,1)}), bf16[2048,3,256]{2,0,1:T(8,128)(2,1)}) %all-gather.7.cloned.1.call-update) | async-done | bytes 3145744 | tf_op jit(solution)/shard_map/all_gather | solution.py:19
  72.0 54.9 %all-gather.5.cloned.1.call-done = bf16[1024,2048]{1,0:T(8,128)(2,1)} async-done(((bf16[128,2048]{1,0:T(8,128)(2,1)}), bf16[1024,2048]{1,0:T(8,128)(2,1)}) %all-gather.5.cloned.1.call-update) | async-done | bytes 4194320 | tf_op jit(solution)/shard_map/all_gather | solution.py:20
  126.9 6.6 fusion.14
  133.5 4.7 collective-permute-start
  138.3 0.8 collective-permute-done
  139.1 0.3 maximum_convert_fusion
  139.4 2.6 multiply_add_fusion
  142.0 1.2 fusion.25
  143.2 2.9 multiply_reduce_fusion
  146.1 1.9 collective-permute-start.1
  148.0 4.8 collective-permute-done.1
  152.8 0.2 pad_maximum_fusion
  153.1 2.7 fusion.8
  155.8 5.1 bitcast_convert_fusion
  160.9 0.0 all-gather.9.cloned.1.call-start
  160.9 53.4 %reduce-scatter.3.cloned.1.call-done = bf16[128,2048]{1,0:T(8,128)(2,1)} async-done(((bf16[1024,2048]{1,0:T(8,128)(2,1)}), bf16[128,2048]{1,0:T(8,128)(2,1)}) %reduce-scatter.3.cloned.1.call-update) | async-done | bytes 524304 | tf_op jit(solution)/shard_map/reduce_scatter | solution.py:56
  214.3 2.0 fusion.29
  216.3 0.2 reduce-scatter.5.cloned.1.call-start
  216.5 7.4 fusion.4
  224.0 137.2 %psum.7 = f32[3,7,256]{2,0,1:T(4,128)S(1)} all-reduce(f32[3,7,256]{2,0,1:T(4,128)S(1)} %constant_dynamic-update-slice_fusion), channel_id=1, replica_groups=mesh['dp'=32,'tensor'=8] {'dp'}, use_global_device_ids=true, to_apply=%region_11.0 | all-reduce | flops 5376 | bytes 43008 | tf_op jit(solution)/shard_map/psum | solution.py:70
  361.3 0.6 copy.16
  361.9 1.1 fusion.23
  363.0 548.0 %all-gather.9.cloned.1.call-done = f32[524288]{0:T(1024)} async-done(((f32[2048]{0:T(1024)}), f32[524288]{0:T(1024)}) %all-gather.9.cloned.1.call-update) | async-done | bytes 2097168 | tf_op jit(solution)/shard_map/all_gather | solution.py:71
  911.0 1.7 reshape.30
  912.8 0.7 reduce_sum.109
  913.5 94.1 %reduce-scatter.5.cloned.1.call-done = bf16[64,3,256]{2,0,1:T(8,128)(2,1)} async-done(((bf16[2048,3,256]{2,0,1:T(8,128)(2,1)}), bf16[64,3,256]{2,0,1:T(8,128)(2,1)}) %reduce-scatter.5.cloned.1.call-update) | async-done | bytes 98320 | tf_op jit(solution)/shard_map/reduce_scatter | solution.py:62
  (30 shorter events, 0.2 us)
Async XLA Ops:
  7.2 64.9 %all-gather.7.cloned.1.call-start = ((), (), s32[]{:S(2)}) async-start(), calls=%async_computation.3 | async-start | bytes 3244032 | tf_op jit(solution)/shard_map/all_gather | solution.py:19
  7.9 119.0 %all-gather.5.cloned.1.call-start = ((), (), s32[]{:S(2)}) async-start(), calls=%async_computation.2 | async-start | bytes 4718592 | tf_op jit(solution)/shard_map/all_gather | solution.py:20
  11.2 203.0 %reduce-scatter.3.cloned.1.call-start = ((), (), s32[]{:S(2)}) async-start(), calls=%async_computation.4 | async-start | bytes 4718592 | tf_op jit(solution)/shard_map/reduce_scatter | solution.py:56
  133.5 5.5 collective-permute-start
  139.4 2.6 copy-start.2
  146.1 6.8 collective-permute-start.1
  153.0 2.7 copy-start.4
  160.8 53.4 %copy-start = (bf16[128,2048]{1,0:T(8,128)(2,1)S(1)}, bf16[128,2048]{1,0:T(8,128)(2,1)}, u32[]{:S(2)}) copy-start(bf16[128,2048]{1,0:T(8,128)(2,1)} %param.5) | copy-start | bytes 1572868
  160.8 53.4 %copy-start.3 = (f32[2048]{0:T(1024)S(1)}, f32[2048]{0:T(1024)}, u32[]{:S(2)}) copy-start(f32[2048]{0:T(1024)} %param.6) | copy-start | bytes 24580
  160.9 750.2 %all-gather.9.cloned.1.call-start = ((), (), s32[]{:S(2)}) async-start(), calls=%async_computation.6 | async-start | bytes 2105344 | tf_op jit(solution)/shard_map/all_gather | solution.py:71
  216.3 791.3 %reduce-scatter.5.cloned.1.call-start = ((), (), s32[]{:S(2)}) async-start(), calls=%async_computation.5 | async-start | bytes 3244032 | tf_op jit(solution)/shard_map/reduce_scatter | solution.py:62
  223.9 138.0 %copy-start.1 = (bf16[128,2048]{1,0:T(8,128)(2,1)S(1)}, bf16[128,2048]{1,0:T(8,128)(2,1)}, u32[]{:S(2)}) copy-start(bf16[128,2048]{1,0:T(8,128)(2,1)} %reduce-scatter.3.cloned.1.call-done) | copy-start | bytes 1572868
Sparse Core Ops, SparseCore 0:
  10.7 61.3 all-gather.6
  74.4 52.5 all-gather.4
  161.0 53.2 reduce-scatter.2
  216.6 694.4 all-gather.8
  915.4 92.1 reduce-scatter.4
